TPU v7x, 256 devices: a whole 4x4x8 slice. The times are simulated.
256 devices in a mesh: rows: 32 (over y, z), grp: 8 (over x, core).
Axes of the slice: x: 4, y: 4, z: 8, core: 2. Of those that a mesh axis runs over, the one named last changes fastest.
Arguments:
- item_table: bfloat16 [507904, 128], P(('rows', 'grp'))
- histories: int32 [16384, 64], P(('rows', 'grp')), may hold values from 0 to 507903, as said below
- counts: int32 [16384], P(('rows', 'grp')), may hold values from 32 to 64
Outputs:
- user_vectors: float32 [16384, 128], P(('rows', 'grp'))
- item_rhs: float32 [507904, 128], P(('rows', 'grp'))
Inputs may be any that keep to these rules, and one draw needn't show every extreme that they name: `histories`: entry j of user u is used only if j < counts[u]. The used entries of the users of one device name items of one owner (rows o * 1984 to (o + 1) * 1984 - 1) at most 32 times, and in every draw some owner is named exactly 32 times by the used entries of every device.
All inputs are finite; a program needn't handle non-finite values.
Results may differ from a plain program's by a relative error of at most 0.0064.
Values may be sent and summed in bfloat16 or wider, within the bound.
No kernel may reach another device: no remote copies, remote signals or barrier semaphores. Data moves between devices by JAX's collectives and lax.ppermute only.
A program may use at most 64 MiB of HBM per device.

v0:
```python
import jax
import jax.numpy as jnp
from jax import lax
from jax.sharding import PartitionSpec as P

ITERS = 3
unobserved_weight = 25.0
ridge = 0.1


def on_device(item_table, histories, counts):
    row_count = lax.axis_size("rows")
    group_count = lax.axis_size("grp")
    devices = row_count * group_count
    table_rows, embed_width = item_table.shape
    user_count, history_length = histories.shape
    lookups = user_count * history_length
    capacity = max(4, 2 * lookups // devices)
    slots_total = devices * capacity
    local_gram = lax.dot_general(
        item_table, item_table, (((0,), (0,)), ((), ())), preferred_element_type=jnp.float32
    )
    gramian = lax.psum(local_gram, ("rows", "grp"))
    positions = lax.broadcasted_iota(jnp.int32, (user_count, history_length), 1)
    live = positions < counts[:, None]
    weights = live.astype(jnp.float32)
    flat_ids = histories.reshape(-1)
    owners = flat_ids // table_rows
    local_rows = flat_ids - owners * table_rows
    owner_key = jnp.where(live.reshape(-1), owners, devices)
    ordering = jnp.argsort(owner_key, stable=True)
    sorted_key = owner_key[ordering]
    starts = jnp.searchsorted(sorted_key, jnp.arange(devices + 1, dtype=jnp.int32), side="left")
    ranks = jnp.arange(lookups, dtype=jnp.int32) - starts[sorted_key]
    sorted_slots = jnp.where(sorted_key < devices, sorted_key * capacity + ranks, slots_total)
    slot_index = jnp.zeros((lookups,), jnp.int32).at[ordering].set(sorted_slots)
    requests = (
        jnp.full((slots_total,), table_rows, jnp.int32).at[slot_index].set(local_rows, mode="drop")
    )
    requests = requests.reshape(row_count, group_count, capacity)
    incoming = lax.all_to_all(
        lax.all_to_all(requests, "grp", split_axis=1, concat_axis=1, tiled=True),
        "rows",
        split_axis=0,
        concat_axis=0,
        tiled=True,
    )
    answered = item_table[jnp.minimum(incoming, table_rows - 1)]
    replies = lax.all_to_all(
        lax.all_to_all(answered, "grp", split_axis=1, concat_axis=1, tiled=True),
        "rows",
        split_axis=0,
        concat_axis=0,
        tiled=True,
    )
    reply_rows = replies.reshape(slots_total, embed_width)
    fetched = reply_rows[jnp.minimum(slot_index, slots_total - 1)].reshape(
        user_count, history_length, embed_width
    )
    narrow_weights = weights.astype(jnp.bfloat16)
    target = jnp.einsum("ul,ulk->uk", narrow_weights, fetched, preferred_element_type=jnp.float32)
    unseen_scale = unobserved_weight / (table_rows * devices)
    solution = jnp.zeros_like(target)
    residual = target
    direction = target
    norm_now = jnp.sum(residual * residual, axis=1)
    for iteration in range(ITERS):
        narrow = direction.astype(jnp.bfloat16)
        scores = jnp.einsum("ulk,uk->ul", fetched, narrow, preferred_element_type=jnp.float32)
        scores = (scores * weights).astype(jnp.bfloat16)
        returned = jnp.einsum("ulk,ul->uk", fetched, scores, preferred_element_type=jnp.float32)
        curved = jnp.dot(direction, gramian, precision=lax.Precision.HIGHEST)
        applied = unseen_scale * curved + returned + ridge * direction
        step_size = norm_now / jnp.sum(direction * applied, axis=1)
        solution = solution + step_size[:, None] * direction
        residual = residual - step_size[:, None] * applied
        norm_next = jnp.sum(residual * residual, axis=1)
        direction = residual + (norm_next / norm_now)[:, None] * direction
        norm_now = norm_next
    repeated = jnp.repeat(solution, history_length, axis=0)
    partials = (
        jnp.zeros((slots_total, embed_width), jnp.float32).at[slot_index].set(repeated, mode="drop")
    )
    partials = partials.reshape(row_count, group_count, capacity, embed_width)
    arrived = lax.all_to_all(
        lax.all_to_all(partials, "grp", split_axis=1, concat_axis=1, tiled=True),
        "rows",
        split_axis=0,
        concat_axis=0,
        tiled=True,
    )
    item_rhs = (
        jnp.zeros((table_rows, embed_width), jnp.float32)
        .at[incoming.reshape(-1)]
        .add(arrived.reshape(-1, embed_width), mode="drop")
    )
    return (solution, item_rhs)


def solution(mesh):
    return jax.shard_map(
        on_device,
        mesh=mesh,
        in_specs=(P(("rows", "grp"), None), P(("rows", "grp"), None), P(("rows", "grp"))),
        out_specs=(P(("rows", "grp"), None), P(("rows", "grp"), None)),
        check_vma=False,
    )
```

profile of v0, /device:TPU:2, one launch (start us, length us, event | category | flops | bytes accessed | tf_op | source)
XLA Modules:
  0.0 701.0 jit_solution(2141229603027904647)
XLA Ops:
  7.2 0.9 reshape.99
  8.1 0.7 fusion.28
  8.8 0.1 lt.63
  8.9 5.8 sort.17
  14.7 23.0 %gather_fusion.1 = s32[4096]{0:T(1024)S(1)} fusion(s32[4096]{0:T(1024)S(1)} %get-tuple-element.108, s32[4096]{0:T(1024)S(1)} %get-tuple-element.109), kind=kCustom, calls=%fused_computation.1 | custom fusion | bytes 49152 | tf_op jit(solution)/shard_map/gather | solution.py:32
  37.8 30.3 %while.24 = (s32[]{:T(128)}, u32[257]{0:T(512)S(1)}, u32[257]{0:T(512)S(1)}, s32[4096]{0:T(1024)S(1)}, s32[]{:T(128)}, /*index=5*/s32[]{:T(128)}, s32[]{}) while((s32[]{:T(128)}, u32[257]{0:T(512)S(1)}, u32[257]{0:T(512)S(1)}, s32[4096]{0:T(1024)S(1)}, s32[]{:T(128)}, /*index=5*/s32[]{:T(128)}, s32[]{}) %tuple.47), condition=%wide.region_2.3_spmd.clone, body=%wide.region_1.2_spmd.clone.sunk | while | flops 5654 | bytes 21159 | solution.py:33
  37.8 2.2 gather_fusion
  40.1 2.2 gather_fusion
  42.5 2.2 gather_fusion
  44.8 2.2 gather_fusion
  47.1 2.2 gather_fusion
  49.4 2.2 gather_fusion
  51.8 2.2 gather_fusion
  54.1 2.2 gather_fusion
  56.4 2.2 gather_fusion
  58.7 2.2 gather_fusion
  61.1 2.2 gather_fusion
  63.4 2.2 gather_fusion
  65.7 2.2 gather_fusion
  68.1 25.9 %gather_fusion.2 = s32[4096]{0:T(1024)S(1)} fusion(s32[257]{0:T(512)S(1)} %convert_element_type.36, s32[4096]{0:T(1024)S(1)} %broadcast_clamp_fusion.1), kind=kCustom, calls=%fused_computation.2 | custom fusion | bytes 49152 | tf_op jit(solution)/shard_map/gather | solution.py:34
  94.0 15.5 %scatter_custom_fusion = s32[4096]{0:T(1024)S(1)} fusion(s32[4096]{0:T(1024)S(1)} %get-tuple-element.110, s32[4096]{0:T(1024)S(1)} %add_select_fusion.1, s32[]{:T(128)} %constant.59.clone.1), kind=kCustom, calls=%fused_computation.85 | custom fusion | bytes 16388 | tf_op jit(solution)/shard_map/scatter | solution.py:36
  109.5 15.5 %scatter_custom_fusion.1 = s32[8192]{0:T(1024)S(1)} fusion(s32[4096]{0:T(1024)S(1)} %get-tuple-element.106, s32[4096]{0:T(1024)S(1)} %get-tuple-element.107, s32[]{:T(128)} %constant.58.clone.1), kind=kCustom, calls=%fused_computation.79 | custom fusion | bytes 32772 | tf_op jit(solution)/shard_map/scatter | solution.py:38
  125.2 0.1 reshape.212
  125.3 8.6 %all_to_all.30 = s32[8,1,1024]{2,1,0:T(1,128)S(1)} all-to-all(s32[8,1,1024]{2,1,0:T(1,128)S(1)} %reshape.212), channel_id=1, replica_groups=mesh['rows'=32,'grp'=8] {'grp'}, dimensions={0} | all-to-all | bytes 65536 | tf_op jit(solution)/shard_map/all_to_all | solution.py:42
  134.0 0.5 broadcast.142
  134.5 0.7 reduce
  135.2 0.1 reshape.213
  135.4 0.1 reshape.214
  135.5 21.2 %all_to_all.31 = s32[32,1,256]{2,1,0:T(1,128)S(1)} all-to-all(s32[32,1,256]{2,1,0:T(1,128)S(1)} %reshape.214), channel_id=1, replica_groups=mesh['rows'=32,'grp'=8] {'rows'}, dimensions={0} | all-to-all | bytes 65536 | tf_op jit(solution)/shard_map/all_to_all | solution.py:41
  156.7 0.7 reduce.1
  157.7 24.0 %gather_fusion.3 = bf16[8192,128]{1,0:T(8,128)(2,1)S(1)} fusion(bf16[1984,128]{1,0:T(8,128)(2,1)S(1)} %copy-done, s32[8192]{0:T(1024)S(1)} %broadcast_clamp_fusion), kind=kCustom, calls=%fused_computation.3 | custom fusion | bytes 4227072 | tf_op jit(solution)/shard_map/gather | solution.py:48
  181.7 0.4 copy.16
  182.2 30.0 %all_to_all.32 = bf16[32,8,32,128]{3,2,0,1:T(8,128)(2,1)S(1)} all-to-all(bf16[32,8,32,128]{3,2,0,1:T(8,128)(2,1)S(1)} %copy.16), channel_id=1, replica_groups=mesh['rows'=32,'grp'=8] {'grp'}, dimensions={1} | all-to-all | bytes 4194304 | tf_op jit(solution)/shard_map/all_to_all | solution.py:50
  212.1 2.0 copy.17
  214.1 4.0 all-to-all-start.3
  218.1 0.2 all-reduce.2.cloned.1.call-start
  218.3 1.0 fusion.38
  219.3 49.0 %all-to-all-done.3 = bf16[32,8,32,128]{3,2,1,0:T(8,128)(2,1)S(1)} async-done(((bf16[32,8,32,128]{3,2,1,0:T(8,128)(2,1)}), bf16[32,8,32,128]{3,2,1,0:T(8,128)(2,1)S(1)}, u32[]{:S(2)}, u32[]{:S(2)}) %all-to-all-start.3) | async-done | bytes 2097184 | tf_op jit(solution)/shard_map/all_to_all | solution.py:49
  268.4 14.9 %gather_fusion.4 = bf16[4096,128]{1,0:T(8,128)(2,1)} fusion(bf16[8192,128]{1,0:T(8,128)(2,1)S(1)} %bitcast.60, s32[4096]{0:T(1024)S(1)} %get-tuple-element.105), kind=kCustom, calls=%fused_computation.4 | custom fusion | bytes 2113536 | tf_op jit(solution)/shard_map/gather | solution.py:57
  283.3 1.7 fusion.26
  285.0 1.9 fusion.24
  286.9 1.6 fusion.22
  288.5 179.1 %all-reduce.2.cloned.1.call-done = f32[128,128]{1,0:T(8,128)} async-done(((f32[128,128]{1,0:T(8,128)}), f32[128,128]{1,0:T(8,128)}) %all-reduce.2.cloned.1.call-update) | async-done | bytes 65552 | tf_op jit(solution)/shard_map/psum | solution.py:23
  467.6 1.2 multiply_reduce_fusion.3
  468.8 0.2 multiply_reduce_fusion.2
  469.0 0.1 convert_bitcast_fusion.1
  469.1 1.9 fusion.20
  471.1 0.4 fusion.18
  471.5 1.1 multiply_reduce_fusion.1
  472.6 0.2 multiply_reduce_fusion
  472.8 0.1 convert_bitcast_fusion
  472.9 0.6 fusion.16
  473.7 0.4 fusion.14
  474.1 0.3 fusion.11
  474.4 0.1 multiply_add_fusion
  474.5 0.1 broadcast_in_dim.68
  474.6 12.8 %scatter_custom_fusion.2 = f32[8192,128]{1,0:T(8,128)} fusion(s32[4096]{0:T(1024)S(1)} %get-tuple-element.106, f32[4096,128]{1,0:T(8,128)S(1)} %bitcast.63, f32[]{:T(128)} %constant.71.clone.1), kind=kCustom, calls=%fused_computation.15 | custom fusion | bytes 4194308 | tf_op jit(solution)/shard_map/scatter | solution.py:82
  487.4 2.8 copy.18
  490.2 53.3 %all_to_all.33 = f32[32,8,32,128]{3,2,0,1:T(8,128)S(1)} all-to-all(f32[32,8,32,128]{3,2,0,1:T(8,128)S(1)} %copy.18), channel_id=1, replica_groups=mesh['rows'=32,'grp'=8] {'grp'}, dimensions={1} | all-to-all | bytes 8388608 | tf_op jit(solution)/shard_map/all_to_all | solution.py:86
  543.5 2.6 copy.19
  546.1 6.1 all-to-all-start.5
  552.2 0.1 reshape.103
  552.4 96.5 %all-to-all-done.5 = f32[32,8,32,128]{3,2,1,0:T(8,128)} async-done(((f32[32,8,32,128]{3,2,1,0:T(8,128)}), f32[32,8,32,128]{3,2,1,0:T(8,128)}, u32[]{:S(2)}, u32[]{:S(2)}) %all-to-all-start.5) | async-done | bytes 4194336 | tf_op jit(solution)/shard_map/all_to_all | solution.py:85
  648.8 45.3 %scatter_custom_fusion.3 = f32[1984,128]{1,0:T(8,128)} fusion(s32[8192]{0:T(1024)S(1)} %bitcast.84, f32[8192,128]{1,0:T(8,128)} %bitcast.29, f32[]{:T(128)} %constant.71.clone.1), kind=kCustom, calls=%fused_computation.28 | custom fusion | flops 1048576 | bytes 1016320 | tf_op jit(solution)/shard_map/scatter-add | solution.py:95
  (103 shorter events, 1.4 us)
Async XLA Ops:
  7.2 150.5 %copy-start = (bf16[1984,128]{1,0:T(8,128)(2,1)S(1)}, bf16[1984,128]{1,0:T(8,128)(2,1)}, u32[]{:S(2)}) copy-start(bf16[1984,128]{1,0:T(8,128)(2,1)} %param.5) | copy-start | bytes 1523716
  214.1 54.3 %all-to-all-start.3 = ((bf16[32,8,32,128]{3,2,1,0:T(8,128)(2,1)}), bf16[32,8,32,128]{3,2,1,0:T(8,128)(2,1)S(1)}, u32[]{:S(2)}, u32[]{:S(2)}) async-start(bf16[32,8,32,128]{3,2,1,0:T(8,128)(2,1)} %copy.17), calls=%async_computation.3 | async-start | bytes 4194304 | tf_op jit(solution)/shard_map/all_to_all | solution.py:49
  218.1 249.5 %all-reduce.2.cloned.1.call-start = ((), (), s32[]{:S(2)}) async-start(), calls=%async_computation.6 | async-start | bytes 131072 | tf_op jit(solution)/shard_map/psum | solution.py:23
  268.4 18.5 %copy-start.4 = (s32[64]{0:T(128)S(1)}, s32[64]{0:T(128)}, u32[]{:S(2)}) copy-start(s32[64]{0:T(128)} %param.7) | copy-start | bytes 772
  283.3 187.8 %copy-start.1 = (bf16[4096,128]{1,0:T(8,128)(2,1)S(1)}, bf16[4096,128]{1,0:T(8,128)(2,1)}, u32[]{:S(2)}) copy-start(bf16[4096,128]{1,0:T(8,128)(2,1)} %gather_fusion.4) | copy-start | bytes 3145732
  467.6 6.4 copy-start.2
  474.5 15.7 %copy-start.3 = (f32[64,128]{1,0:T(8,128)}, f32[64,128]{1,0:T(8,128)S(1)}, u32[]{:S(2)}) copy-start(f32[64,128]{1,0:T(8,128)S(1)} %multiply_add_fusion) | copy-start | bytes 98308
  546.1 102.8 %all-to-all-start.5 = ((f32[32,8,32,128]{3,2,1,0:T(8,128)}), f32[32,8,32,128]{3,2,1,0:T(8,128)}, u32[]{:S(2)}, u32[]{:S(2)}) async-start(f32[32,8,32,128]{3,2,1,0:T(8,128)} %copy.19), calls=%async_computation.5 | async-start | bytes 8388608 | tf_op jit(solution)/shard_map/all_to_all | solution.py:85
Sparse Core Ops, SparseCore 0:
  225.0 242.5 all-reduce.1
where the time goes:
time: 702 us; the launch traced here: 701 us
  waiting for transfers between devices  325 us (46%)
  local copies, waits for them, and re-layouts  171 us (24%)
  blocking collectives  113 us (16%)
  other arithmetic  54.8 us (8%)
  between operations  14.4 us (2%)
  matrix products  12 us (2%)
  starting transfers between devices  10.4 us (1%)
    psum x1, waiting for transfers between devices, on_device(): gramian = lax.psum(local_gram, ('rows', 'grp'))  179 us
    all_to_all x1, waiting for transfers between devices, on_device(): lax.all_to_all(lax.all_to_all(partials, 'grp', split_axis=1, concat_axis=...  96.5 us
    all_to_all x1, blocking collectives, on_device(): lax.all_to_all(partials, 'grp', split_axis=1, concat_axis=1, tiled=True)  53.3 us
    all_to_all x1, waiting for transfers between devices, on_device(): lax.all_to_all(lax.all_to_all(answered, 'grp', split_axis=1, concat_axis=...  49 us
    scatter-add x1, other arithmetic, on_device(): item_rhs = jnp.zeros((table_rows, embed_width), jnp.float32).at[incoming....  45.3 us
    all_to_all x1, blocking collectives, on_device(): lax.all_to_all(answered, 'grp', split_axis=1, concat_axis=1, tiled=True)  30 us
    gather x13, local copies, waits for them, and re-layouts, on_device(): jnp.searchsorted(sorted_key, jnp.arange(devices + 1, dtype=jnp.int32), si...  29 us
    gather x1, local copies, waits for them, and re-layouts, on_device(): ranks = jnp.arange(lookups, dtype=jnp.int32) - starts[sorted_key]  25.9 us
  transfers between devices with their start and end apart: 3, of which 3 were waited for; matrix products, arithmetic and copies ran while one was open for 3% of the time, Pallas kernels for 0%

commit v1 on v0

--- a/solution.py
+++ b/solution.py
@@ -6,6 +6,12 @@
 ITERS = 3
 unobserved_weight = 25.0
 ridge = 0.1
+
+
+def summed_here(x, axis):
+    parts = lax.all_gather(x, axis, axis=0, tiled=False)
+    total = parts.sum(axis=0)
+    return total
 
 
 def on_device(item_table, histories, counts):
@@ -20,7 +26,7 @@
     local_gram = lax.dot_general(
         item_table, item_table, (((0,), (0,)), ((), ())), preferred_element_type=jnp.float32
     )
-    gramian = lax.psum(local_gram, ("rows", "grp"))
+    gramian = summed_here(local_gram, ("rows", "grp"))
     positions = lax.broadcasted_iota(jnp.int32, (user_count, history_length), 1)
     live = positions < counts[:, None]
     weights = live.astype(jnp.float32)

time: 702 us -> 525 us (0.75)
  waiting for transfers between devices: 325 us -> 96.5 us
  blocking collectives: 113 us -> 167 us
    psum x1 -> x0, waiting for transfers between devices: 179 us -> none  [on_device(): gramian = lax.psum(local_gram, ('rows', 'grp'))]
    all_to_all x0 -> x1, blocking collectives: none -> 54.1 us  [on_device(): lax.all_to_all(lax.all_to_all(answered, 'grp', split_axis=1, concat_axis=...]
    all_to_all x1 -> x0, waiting for transfers between devices: 49 us -> none  [on_device(): lax.all_to_all(lax.all_to_all(answered, 'grp', split_axis=1, concat_axis=...]
  transfers between devices with their start and end apart: 3 -> 2, of which waited for: 3 -> 1; matrix products, arithmetic and copies ran while one was open for 3% -> 31% of each run, Pallas kernels for 0% -> 0%
where the time goes in v1:
time: 525 us; the launch traced here: 524 us
  local copies, waits for them, and re-layouts  171 us (33%)
  blocking collectives  167 us (32%)
  waiting for transfers between devices  96.5 us (18%)
  other arithmetic  61.5 us (12%)
  between operations  14.4 us (3%)
  matrix products  8.99 us (2%)
    all_to_all x1, waiting for transfers between devices, on_device(): lax.all_to_all(lax.all_to_all(partials, 'grp', split_axis=1, concat_axis=...  96.5 us
    all_to_all x1, blocking collectives, on_device(): lax.all_to_all(lax.all_to_all(answered, 'grp', split_axis=1, concat_axis=...  54.1 us
    all_to_all x1, blocking collectives, on_device(): lax.all_to_all(partials, 'grp', split_axis=1, concat_axis=1, tiled=True)  52.8 us
    scatter-add x1, other arithmetic, on_device(): item_rhs = jnp.zeros((table_rows, embed_width), jnp.float32).at[incoming....  45.3 us
    all_to_all x1, blocking collectives, on_device(): lax.all_to_all(answered, 'grp', split_axis=1, concat_axis=1, tiled=True)  30 us
    gather x13, local copies, waits for them, and re-layouts, on_device(): jnp.searchsorted(sorted_key, jnp.arange(devices + 1, dtype=jnp.int32), si...  29 us
    gather x1, local copies, waits for them, and re-layouts, on_device(): ranks = jnp.arange(lookups, dtype=jnp.int32) - starts[sorted_key]  25.9 us
    gather x2, local copies, waits for them, and re-layouts, on_device(): answered = item_table[jnp.minimum(incoming, table_rows - 1)]  24.5 us
  transfers between devices with their start and end apart: 2, of which 1 were waited for; matrix products, arithmetic and copies ran while one was open for 31% of the time, Pallas kernels for 0%

profile of v1, /device:TPU:2, one launch (start us, length us, event | category | flops | bytes accessed | tf_op | source)
XLA Modules:
  0.0 524.5 jit_solution(8467153001578466144)
XLA Ops:
  7.2 1.0 copy-done
  8.2 1.0 fusion.38
  9.2 0.8 reshape.99
  10.1 0.7 fusion.28
  10.8 0.1 lt.63
  10.9 5.8 %sort.17 = (s32[4096]{0:T(1024)}, s32[4096]{0:T(1024)S(1)}) sort(s32[4096]{0:T(1024)S(1)} %get-tuple-element.108, s32[4096]{0:T(1024)S(1)} %iota.18), dimensions={0}, to_apply=%region_0.0 | sort | flops 49152 | bytes 65536 | tf_op jit(solution)/shard_map/jit(argsort)/sort | solution.py:37
  16.7 23.0 %gather_fusion.1 = s32[4096]{0:T(1024)S(1)} fusion(s32[4096]{0:T(1024)S(1)} %get-tuple-element.108, s32[4096]{0:T(1024)S(1)} %get-tuple-element.109), kind=kCustom, calls=%fused_computation.1 | custom fusion | bytes 49152 | tf_op jit(solution)/shard_map/gather | solution.py:38
  39.7 30.3 %while.24 = (s32[]{:T(128)}, u32[257]{0:T(512)S(1)}, u32[257]{0:T(512)S(1)}, s32[4096]{0:T(1024)S(1)}, s32[]{:T(128)}, /*index=5*/s32[]{:T(128)}, s32[]{}) while((s32[]{:T(128)}, u32[257]{0:T(512)S(1)}, u32[257]{0:T(512)S(1)}, s32[4096]{0:T(1024)S(1)}, s32[]{:T(128)}, /*index=5*/s32[]{:T(128)}, s32[]{}) %tuple.47), condition=%wide.region_2.3_spmd.clone, body=%wide.region_1.2_spmd.clone.sunk | while | flops 5654 | bytes 21159 | solution.py:39
  39.8 2.2 gather_fusion
  42.1 2.2 gather_fusion
  44.4 2.2 gather_fusion
  46.8 2.2 gather_fusion
  49.1 2.2 gather_fusion
  51.4 2.2 gather_fusion
  53.7 2.2 gather_fusion
  56.1 2.2 gather_fusion
  58.4 2.2 gather_fusion
  60.7 2.2 gather_fusion
  63.0 2.2 gather_fusion
  65.4 2.2 gather_fusion
  67.7 2.2 gather_fusion
  70.0 25.9 %gather_fusion.2 = s32[4096]{0:T(1024)S(1)} fusion(s32[257]{0:T(512)S(1)} %convert_element_type.36, s32[4096]{0:T(1024)S(1)} %broadcast_clamp_fusion.1), kind=kCustom, calls=%fused_computation.2 | custom fusion | bytes 49152 | tf_op jit(solution)/shard_map/gather | solution.py:40
  96.0 15.5 %scatter_custom_fusion = s32[4096]{0:T(1024)S(1)} fusion(s32[4096]{0:T(1024)S(1)} %get-tuple-element.110, s32[4096]{0:T(1024)S(1)} %add_select_fusion.1, s32[]{:T(128)} %constant.59.clone.1), kind=kCustom, calls=%fused_computation.85 | custom fusion | bytes 16388 | tf_op jit(solution)/shard_map/scatter | solution.py:42
  111.5 15.5 %scatter_custom_fusion.1 = s32[8192]{0:T(1024)S(1)} fusion(s32[4096]{0:T(1024)S(1)} %get-tuple-element.106, s32[4096]{0:T(1024)S(1)} %get-tuple-element.107, s32[]{:T(128)} %constant.58.clone.1), kind=kCustom, calls=%fused_computation.79 | custom fusion | bytes 32772 | tf_op jit(solution)/shard_map/scatter | solution.py:44
  127.2 0.1 reshape.213
  127.3 8.6 %all_to_all.30 = s32[8,1,1024]{2,1,0:T(1,128)S(1)} all-to-all(s32[8,1,1024]{2,1,0:T(1,128)S(1)} %reshape.213), channel_id=1, replica_groups=mesh['rows'=32,'grp'=8] {'grp'}, dimensions={0} | all-to-all | bytes 65536 | tf_op jit(solution)/shard_map/all_to_all | solution.py:48
  135.9 0.5 broadcast.142
  136.4 0.7 reduce
  137.2 0.1 reshape.214
  137.4 0.1 reshape.215
  137.5 21.2 %all_to_all.31 = s32[32,1,256]{2,1,0:T(1,128)S(1)} all-to-all(s32[32,1,256]{2,1,0:T(1,128)S(1)} %reshape.215), channel_id=1, replica_groups=mesh['rows'=32,'grp'=8] {'rows'}, dimensions={0} | all-to-all | bytes 65536 | tf_op jit(solution)/shard_map/all_to_all | solution.py:47
  158.7 0.7 reduce.1
  159.5 0.1 reshape.133
  159.6 24.0 %gather_fusion.3 = bf16[8192,128]{1,0:T(8,128)(2,1)S(1)} fusion(bf16[1984,128]{1,0:T(8,128)(2,1)S(1)} %copy-done, s32[8192]{0:T(1024)S(1)} %broadcast_clamp_fusion), kind=kCustom, calls=%fused_computation.3 | custom fusion | bytes 4227072 | tf_op jit(solution)/shard_map/gather | solution.py:54
  183.7 0.4 copy.16
  184.1 30.0 %all_to_all.32 = bf16[32,8,32,128]{3,2,0,1:T(8,128)(2,1)S(1)} all-to-all(bf16[32,8,32,128]{3,2,0,1:T(8,128)(2,1)S(1)} %copy.16), channel_id=1, replica_groups=mesh['rows'=32,'grp'=8] {'grp'}, dimensions={1} | all-to-all | bytes 4194304 | tf_op jit(solution)/shard_map/all_to_all | solution.py:56
  214.1 0.6 copy.17
  214.7 54.1 %all_to_all.33 = bf16[32,8,32,128]{3,2,1,0:T(8,128)(2,1)S(1)} all-to-all(bf16[32,8,32,128]{3,2,1,0:T(8,128)(2,1)S(1)} %copy.17), channel_id=1, replica_groups=mesh['rows'=32,'grp'=8] {'rows'}, dimensions={0} | all-to-all | bytes 4194304 | tf_op jit(solution)/shard_map/all_to_all | solution.py:55
  268.8 14.9 %gather_fusion.4 = bf16[4096,128]{1,0:T(8,128)(2,1)} fusion(bf16[8192,128]{1,0:T(8,128)(2,1)S(1)} %bitcast.61, s32[4096]{0:T(1024)S(1)} %get-tuple-element.105), kind=kCustom, calls=%fused_computation.4 | custom fusion | bytes 2113536 | tf_op jit(solution)/shard_map/gather | solution.py:63
  283.7 1.6 fusion.26
  285.3 1.9 fusion.24
  287.2 1.6 fusion.22
  288.9 6.7 %reduce_sum.64 = f32[128,128]{1,0:T(8,128)S(1)} reduce(f32[256,128,128]{2,1,0:T(8,128)} %bitcast.62, f32[]{:T(128)} %constant.71.clone.1), dimensions={0}, to_apply=%region_6.7 | reduce | flops 4177920 | bytes 16842756 | tf_op jit(solution)/shard_map/reduce_sum | solution.py:13
  295.6 0.3 multiply_reduce_fusion.3
  295.9 0.2 multiply_reduce_fusion.2
  296.1 0.1 convert_bitcast_fusion.1
  296.2 0.6 fusion.20
  296.9 0.4 fusion.18
  297.3 0.3 multiply_reduce_fusion.1
  297.6 0.2 multiply_reduce_fusion
  297.8 0.1 convert_bitcast_fusion
  297.9 0.6 fusion.16
  298.6 0.4 fusion.14
  299.0 0.3 fusion.11
  299.3 0.1 multiply_add_fusion
  299.4 0.1 broadcast_in_dim.68
  299.6 12.8 %scatter_custom_fusion.2 = f32[8192,128]{1,0:T(8,128)} fusion(s32[4096]{0:T(1024)S(1)} %get-tuple-element.106, f32[4096,128]{1,0:T(8,128)S(1)} %bitcast.65, f32[]{:T(128)} %constant.71.clone.1), kind=kCustom, calls=%fused_computation.15 | custom fusion | bytes 4194308 | tf_op jit(solution)/shard_map/scatter | solution.py:88
  312.3 2.8 copy.18
  315.1 52.8 %all_to_all.34 = f32[32,8,32,128]{3,2,0,1:T(8,128)S(1)} all-to-all(f32[32,8,32,128]{3,2,0,1:T(8,128)S(1)} %copy.18), channel_id=1, replica_groups=mesh['rows'=32,'grp'=8] {'grp'}, dimensions={1} | all-to-all | bytes 8388608 | tf_op jit(solution)/shard_map/all_to_all | solution.py:92
  368.0 2.6 copy.19
  370.6 5.2 all-to-all-start.5
  375.7 0.1 reshape.103
  375.9 96.5 %all-to-all-done.5 = f32[32,8,32,128]{3,2,1,0:T(8,128)} async-done(((f32[32,8,32,128]{3,2,1,0:T(8,128)}), f32[32,8,32,128]{3,2,1,0:T(8,128)}, u32[]{:S(2)}, u32[]{:S(2)}) %all-to-all-start.5) | async-done | bytes 4194336 | tf_op jit(solution)/shard_map/all_to_all | solution.py:91
  472.4 45.3 %scatter_custom_fusion.3 = f32[1984,128]{1,0:T(8,128)} fusion(s32[8192]{0:T(1024)S(1)} %bitcast.86, f32[8192,128]{1,0:T(8,128)} %bitcast.30, f32[]{:T(128)} %constant.71.clone.1), kind=kCustom, calls=%fused_computation.28 | custom fusion | flops 1048576 | bytes 1016320 | tf_op jit(solution)/shard_map/scatter-add | solution.py:101
  (101 shorter events, 1.3 us)
Async XLA Ops:
  7.2 1.0 copy-start
  7.2 281.7 %all-gather.3.cloned.1.call-start = ((), (), s32[]{:S(2)}) async-start(), calls=%async_computation.6 | async-start | bytes 16842752 | tf_op jit(solution)/shard_map/all_gather | solution.py:12
  268.8 18.4 %copy-start.3 = (s32[64]{0:T(128)S(1)}, s32[64]{0:T(128)}, u32[]{:S(2)}) copy-start(s32[64]{0:T(128)} %param.7) | copy-start | bytes 772
  288.9 7.3 %copy-start.1 = (bf16[4096,128]{1,0:T(8,128)(2,1)S(1)}, bf16[4096,128]{1,0:T(8,128)(2,1)}, u32[]{:S(2)}) copy-start(bf16[4096,128]{1,0:T(8,128)(2,1)} %gather_fusion.4) | copy-start | bytes 3145732
  299.4 15.7 %copy-start.2 = (f32[64,128]{1,0:T(8,128)}, f32[64,128]{1,0:T(8,128)S(1)}, u32[]{:S(2)}) copy-start(f32[64,128]{1,0:T(8,128)S(1)} %multiply_add_fusion) | copy-start | bytes 98308
  370.6 101.8 %all-to-all-start.5 = ((f32[32,8,32,128]{3,2,1,0:T(8,128)}), f32[32,8,32,128]{3,2,1,0:T(8,128)}, u32[]{:S(2)}, u32[]{:S(2)}) async-start(f32[32,8,32,128]{3,2,1,0:T(8,128)} %copy.19), calls=%async_computation.5 | async-start | bytes 8388608 | tf_op jit(solution)/shard_map/all_to_all | solution.py:91
Sparse Core Ops, SparseCore 0:
  12.2 127.7 all-gather.2
